TPU v7x, 512 devices: a whole 4x4x16 slice. The times are simulated.
512 devices in a mesh: req: 128 (over z, y, core), tp: 4 (over x).
Axes of the slice: x: 4, y: 4, z: 16, core: 2. Of those that a mesh axis runs over, the one named last changes fastest.
Arguments:
- states: bfloat16 [32768, 3072], P('req', 'tp'), may hold values from -12 to 12
- query_weight: bfloat16 [3072, 1536], P(None, 'tp'), may hold values from -0.75 to 0.75
- key_value_weight: bfloat16 [3072, 512], P(None, 'tp'), may hold values from -0.75 to 0.75
- lengths: int32 [128], P('req'), may hold values from 1 to 256, 16384 in all
- adapter_ids: int32 [128], P('req'), may hold values from 0 to 63, as said below
- adapter_slot: int32 [64], replicated, may hold values from 0 to 127, as said below
- down_store: bfloat16 [128, 3072, 32], P('req', 'tp'), may hold values from -0.109375 to 0.109375
- query_up_store: bfloat16 [128, 16, 1536], P('req', None, 'tp'), may hold values from -1.5 to 1.5
- key_value_store: bfloat16 [128, 16, 512], P('req', None, 'tp'), may hold values from -1.5 to 1.5
Outputs:
- context: bfloat16 [32768, 1536], P('req', 'tp')
Inputs may be any that keep to these rules, and one draw needn't show every extreme that they name: `adapter_ids`: exactly 16 distinct adapters are named among all 128 requests. `adapter_slot`: distinct adapters have distinct rows.
All inputs are finite; a program needn't handle non-finite values. No bound on the sum of `lengths` on one device may be relied on, other than what follows from the above.
Results may differ from a plain program's by a relative error of at most 0.0072.
Values may be sent and summed in bfloat16 or wider, within the bound.
No kernel may reach another device: no remote copies, remote signals or barrier semaphores. Data moves between devices by JAX's collectives and lax.ppermute only.
A program may use at most 64 MiB of HBM per device.

v0:
```python
import math
import jax
import jax.numpy as jnp
from jax import lax
from jax.sharding import PartitionSpec as P

HEADS = 12
HEAD_DIM = 128
adapter_scale = 0.5
rope_base = 100000000000.0


def rotate(field):
    half = field.shape[-1] // 2
    count = field.shape[-3]
    position = jnp.arange(count).astype(jnp.float32)
    inverse = rope_base ** (-(jnp.arange(half).astype(jnp.float32) * 2.0) / field.shape[-1])
    angle = position[:, None] * inverse[None, :]
    cosine = jnp.cos(angle)[:, None, :]
    sine = jnp.sin(angle)[:, None, :]
    first_half = field[..., :half]
    second_half = field[..., half:]
    return jnp.concatenate(
        [first_half * cosine - second_half * sine, second_half * cosine + first_half * sine],
        axis=-1,
    )


def lookup_slots(wanted, adapter_slot):
    table = jnp.arange(adapter_slot.shape[0], dtype=jnp.int32)
    matches = wanted[:, None] == table[None, :]
    return jnp.sum(jnp.where(matches, adapter_slot[None, :], 0), axis=1)


def local(
    states,
    query_weight,
    key_value_weight,
    lengths,
    adapter_ids,
    adapter_slot,
    down_store,
    query_up_store,
    key_value_store,
):
    tp_index = lax.axis_index("tp")
    req_dev = lengths.shape[0]
    rows_total = states.shape[0]
    slot_len = rows_total // req_dev
    q_cols = query_weight.shape[1]
    kv_cols = key_value_weight.shape[1]
    heads_here = q_cols // HEAD_DIM
    pooled = (
        lax.all_gather(down_store, "req", axis=0, tiled=True),
        lax.all_gather(query_up_store, "req", axis=0, tiled=True),
        lax.all_gather(key_value_store, "req", axis=0, tiled=True),
    )
    own_slots = lookup_slots(adapter_ids, adapter_slot)
    adapter_down, adapter_query, adapter_pair = (
        jnp.take(member, own_slots, axis=0) for member in pooled
    )
    full_down = lax.all_gather(adapter_down, "tp", axis=1, tiled=True)
    piece = lax.all_gather(states, "tp", axis=1, tiled=True)
    width = piece.shape[1]
    grouped = piece.reshape(req_dev, slot_len, width)
    query_total = jnp.dot(piece, query_weight, preferred_element_type=jnp.float32)
    key_value_sum = jnp.dot(piece, key_value_weight, preferred_element_type=jnp.float32)
    rank_sum = jnp.einsum("rsd,rdk->rsk", grouped, full_down, preferred_element_type=jnp.float32)
    rank_mid = rank_sum.astype(jnp.bfloat16)
    rank_cols = rank_mid.shape[2] // 2
    query_addition = jnp.einsum(
        "rsk,rkc->rsc",
        rank_mid[:, :, :rank_cols],
        adapter_query,
        preferred_element_type=jnp.float32,
    ).reshape(rows_total, q_cols)
    key_value_extra = jnp.einsum(
        "rsk,rkc->rsc", rank_mid[:, :, rank_cols:], adapter_pair, preferred_element_type=jnp.float32
    ).reshape(rows_total, kv_cols)
    query_plain = query_total + adapter_scale * query_addition
    key_value_own = (key_value_sum + adapter_scale * key_value_extra).astype(jnp.bfloat16)
    pair_all = lax.all_gather(key_value_own, "tp", axis=1, tiled=True)
    key_width = pair_all.shape[1] // 2
    kv_heads = key_width // HEAD_DIM
    group = HEADS // kv_heads
    kv_index = tp_index * heads_here // group
    key_block = lax.dynamic_slice_in_dim(pair_all, kv_index * HEAD_DIM, HEAD_DIM, 1)
    value_block = lax.dynamic_slice_in_dim(pair_all, key_width + kv_index * HEAD_DIM, HEAD_DIM, 1)
    queries = rotate(query_plain.reshape(req_dev, slot_len, heads_here, HEAD_DIM)).astype(
        jnp.bfloat16
    )
    keys_one = rotate(key_block.astype(jnp.float32).reshape(req_dev, slot_len, 1, HEAD_DIM)).astype(
        jnp.bfloat16
    )[:, :, 0, :]
    values_one = value_block.reshape(req_dev, slot_len, HEAD_DIM)
    scale = 1.0 / math.sqrt(HEAD_DIM)
    scores = (
        jnp.einsum("rqhd,rkd->rhqk", queries, keys_one, preferred_element_type=jnp.float32) * scale
    )
    position = jnp.arange(slot_len, dtype=jnp.int32)
    allowed = (position[None, None, :] <= position[None, :, None]) & (
        position[None, None, :] < lengths[:, None, None]
    )
    scores = jnp.where(allowed[:, None, :, :], scores, -jnp.inf)
    highest = jnp.max(scores, axis=-1, keepdims=True)
    expo = jnp.exp(scores - highest)
    weights = (expo / jnp.sum(expo, axis=-1, keepdims=True)).astype(jnp.bfloat16)
    context = jnp.einsum("rhqk,rkd->rqhd", weights, values_one, preferred_element_type=jnp.float32)
    live_rows = position[None, :] < lengths[:, None]
    context = jnp.where(live_rows[:, :, None, None], context, 0.0)
    return context.reshape(rows_total, q_cols).astype(jnp.bfloat16)


def solution(mesh):
    return jax.shard_map(
        local,
        mesh=mesh,
        in_specs=(
            P("req", "tp"),
            P(None, "tp"),
            P(None, "tp"),
            P("req"),
            P("req"),
            P(),
            P("req", "tp", None),
            P("req", None, "tp"),
            P("req", None, "tp"),
        ),
        out_specs=P("req", "tp"),
        check_vma=False,
    )
```

profile of v0, /device:TPU:2, one launch (start us, length us, event | category | flops | bytes accessed | tf_op | source)
XLA Modules:
  0.0 358.5 jit_solution(2716103049818812552)
XLA Ops:
  6.5 0.0 copy-start
  6.5 0.7 all-gather.4.cloned.1.call-update
  7.3 0.0 all-gather.6.cloned.1.call-start
  7.3 0.7 all-gather.6.cloned.1.call-update
  8.0 0.0 all-gather.8.cloned.1.call-start
  8.1 0.7 all-gather.8.cloned.1.call-update
  9.4 1.3 fusion.39
  13.4 0.0 copy-start.6
  13.4 96.3 %all_gather.21 = bf16[128,16,128]{2,1,0:T(8,128)(2,1)} all-gather(bf16[1,16,128]{2,1,0:T(8,128)(2,1)} %param.17), channel_id=1, replica_groups=mesh['req'=128,'tp'=4] {'req'}, dimensions={0}, use_global_device_ids=true | all-gather | bytes 528384 | tf_op jit(solution)/shard_map/all_gather | solution.py:56
  109.7 0.1 fusion.9
  109.8 1.2 multiply_cosine_fusion
  111.0 2.4 fusion.45
  113.4 82.7 %all-gather.6.cloned.1.call-done = bf16[128,768,32]{1,2,0:T(8,128)(2,1)} async-done(((bf16[1,768,32]{1,2,0:T(8,128)(2,1)}), bf16[128,768,32]{1,2,0:T(8,128)(2,1)}) %all-gather.6.cloned.1.call-update) | async-done | bytes 6291472 | tf_op jit(solution)/shard_map/all_gather | solution.py:54
  196.1 0.8 dynamic-slice_select_fusion
  196.9 12.4 %all_gather.20 = bf16[1,3072,32]{1,2,0:T(8,128)(2,1)S(1)} all-gather(bf16[1,768,32]{1,2,0:T(8,128)(2,1)S(1)} %dynamic-slice_select_fusion), channel_id=1, replica_groups=mesh['req'=128,'tp'=4] {'tp'}, dimensions={1}, use_global_device_ids=true | all-gather | bytes 245760 | tf_op jit(solution)/shard_map/all_gather | solution.py:62
  209.3 2.0 fusion.6
  211.2 121.7 %all-gather.8.cloned.1.call-done = bf16[128,16,384]{2,1,0:T(8,128)(2,1)} async-done(((bf16[1,16,384]{2,1,0:T(8,128)(2,1)}), bf16[128,16,384]{2,1,0:T(8,128)(2,1)}) %all-gather.8.cloned.1.call-update) | async-done | bytes 1572880 | tf_op jit(solution)/shard_map/all_gather | solution.py:55
  332.9 1.0 fusion.2
  333.9 0.2 copy.21
  334.1 0.2 copy.30
  334.3 0.2 copy.31
  334.4 0.9 convolution_multiply_fusion.2
  335.4 0.0 copy-start.1
  335.4 2.2 fusion.5
  337.6 12.0 %all_gather.22 = bf16[256,512]{1,0:T(8,128)(2,1)S(1)} all-gather(bf16[256,128]{1,0:T(8,128)(2,1)S(1)} %fusion.5), channel_id=1, replica_groups=mesh['req'=128,'tp'=4] {'tp'}, dimensions={1}, use_global_device_ids=true | all-gather | bytes 327680 | tf_op jit(solution)/shard_map/all_gather | solution.py:82
  349.6 0.6 fusion.29
  350.2 0.1 fusion.10
  350.4 0.4 fusion.44
  350.7 0.1 fusion.7
  350.9 0.0 copy-done.7
  350.9 0.3 fusion.4
  351.2 0.8 copy.26
  (19 shorter events, 0.1 us)
Async XLA Ops:
  6.5 104.5 %copy-start = (bf16[3072,384]{1,0:T(8,128)(2,1)S(1)}, bf16[3072,384]{1,0:T(8,128)(2,1)}, u32[]{:S(2)}) copy-start(bf16[3072,384]{1,0:T(8,128)(2,1)} %param.10) | copy-start | bytes 7077892
  6.5 104.5 %all-gather.4.cloned.1.call-start = ((), (), s32[]{:S(2)}) async-start(), calls=%async_computation | async-start | bytes 1966080 | tf_op jit(solution)/shard_map/all_gather | solution.py:63
  7.3 188.8 %all-gather.6.cloned.1.call-start = ((), (), s32[]{:S(2)}) async-start(), calls=%async_computation.1 | async-start | bytes 6340608 | tf_op jit(solution)/shard_map/all_gather | solution.py:54
  8.0 324.9 %all-gather.8.cloned.1.call-start = ((), (), s32[]{:S(2)}) async-start(), calls=%async_computation.2 | async-start | bytes 1585152 | tf_op jit(solution)/shard_map/all_gather | solution.py:55
  13.3 96.5 %copy-start.4 = (f32[64]{0:T(128)}, f32[64]{0:T(128)S(1)}, u32[]{:S(2)}) copy-start(f32[64]{0:T(128)S(1)} %multiply_power_fusion) | copy-start | bytes 772
  13.4 96.3 %copy-start.6 = (pred[256]{0:T(512)(128)(4,1)}, pred[256]{0:T(512)(128)(4,1)S(1)}, u32[]{:S(2)}) copy-start(pred[256]{0:T(512)(128)(4,1)S(1)} %iota_compare_fusion.1) | copy-start | bytes 772
  13.4 96.4 %copy-start.2 = (f32[256]{0:T(256)}, f32[256]{0:T(256)S(1)}, u32[]{:S(2)}) copy-start(f32[256]{0:T(256)S(1)} %iota_convert_fusion) | copy-start | bytes 3076
  335.3 14.3 %copy-start.3 = (f32[256]{0:T(256)S(1)}, f32[256]{0:T(256)}, u32[]{:S(2)}) copy-start(f32[256]{0:T(256)} %copy-done.2) | copy-start | bytes 3076
  335.3 14.3 %copy-start.5 = (f32[64]{0:T(128)S(1)}, f32[64]{0:T(128)}, u32[]{:S(2)}) copy-start(f32[64]{0:T(128)} %copy-done.4) | copy-start | bytes 772
  335.4 14.9 %copy-start.1 = (f32[256,64]{1,0:T(8,128)S(1)}, f32[256,64]{1,0:T(8,128)}, u32[]{:S(2)}) copy-start(f32[256,64]{1,0:T(8,128)} %get-tuple-element.45) | copy-start | bytes 196612
  350.2 0.7 copy-start.7
Sparse Core Ops, SparseCore 0:
  9.5 37.5 all-gather.3
  50.2 145.7 all-gather.5
  199.1 133.7 all-gather.7
where the time goes:
time: 359 us
  waiting for transfers between devices  206 us (57%)
  blocking collectives  121 us (34%)
  between operations  16.5 us (5%)
  matrix products  9.02 us (3%)
  other arithmetic  4.29 us (1%)
    all_gather x1, waiting for transfers between devices, local(): lax.all_gather(query_up_store, 'req', axis=0, tiled=True)  122 us
    all_gather x1, blocking collectives, local(): lax.all_gather(key_value_store, 'req', axis=0, tiled=True)  96.3 us
    all_gather x1, waiting for transfers between devices, local(): lax.all_gather(down_store, 'req', axis=0, tiled=True)  82.7 us
    all_gather x1, blocking collectives, local(): full_down = lax.all_gather(adapter_down, 'tp', axis=1, tiled=True)  12.4 us
    all_gather x1, blocking collectives, local(): pair_all = lax.all_gather(key_value_own, 'tp', axis=1, tiled=True)  12 us
  transfers between devices with their start and end apart: 3, of which 2 were waited for; matrix products, arithmetic and copies ran while one was open for 2% of the time, Pallas kernels for 0%

commit v1 on v0

--- a/solution.py
+++ b/solution.py
@@ -52,7 +52,9 @@
     heads_here = q_cols // HEAD_DIM
     pooled = (
         lax.all_gather(down_store, "req", axis=0, tiled=True),
-        lax.all_gather(query_up_store, "req", axis=0, tiled=True),
+        jnp.concatenate(
+            lax.all_to_all(jnp.stack([query_up_store] * lax.axis_size("req")), "req", 0, 0), axis=0
+        ),
         lax.all_gather(key_value_store, "req", axis=0, tiled=True),
     )
     own_slots = lookup_slots(adapter_ids, adapter_slot)

time: 359 us -> 242 us (0.67)
  waiting for transfers between devices: 206 us -> 16.2 us
  blocking collectives: 121 us -> 172 us
  starting transfers between devices: 0.08 us -> 20.6 us
    all_gather x1 -> x0, waiting for transfers between devices: 122 us -> none  [local(): lax.all_gather(query_up_store, 'req', axis=0, tiled=True)]
    all_gather x1, waiting for transfers between devices: 82.7 us -> 14.7 us  [local(): lax.all_gather(down_store, 'req', axis=0, tiled=True)]
    all_gather x1, blocking collectives: 96.3 us -> 148 us  [local(): lax.all_gather(key_value_store, 'req', axis=0, tiled=True)]
    all_to_all x0 -> x1, starting transfers between devices: none -> 20.6 us  [local(): lax.all_to_all(jnp.stack([query_up_store] * lax.axis_size('req')), 'req',...]
  transfers between devices with their start and end apart: 3 -> 3, of which waited for: 2 -> 1; matrix products, arithmetic and copies ran while one was open for 2% -> 4% of each run, Pallas kernels for 0% -> 0%
where the time goes in v1:
time: 242 us
  blocking collectives  172 us (71%)
  starting transfers between devices  20.6 us (9%)
  between operations  17 us (7%)
  waiting for transfers between devices  16.2 us (7%)
  matrix products  9.05 us (4%)
  other arithmetic  3.64 us (2%)
  local copies, waits for them, and re-layouts  3.38 us (1%)
    all_gather x1, blocking collectives, local(): lax.all_gather(key_value_store, 'req', axis=0, tiled=True)  148 us
    all_to_all x1, starting transfers between devices, local(): lax.all_to_all(jnp.stack([query_up_store] * lax.axis_size('req')), 'req',...  20.6 us
    all_gather x1, waiting for transfers between devices, local(): lax.all_gather(down_store, 'req', axis=0, tiled=True)  14.7 us
    all_gather x1, blocking collectives, local(): full_down = lax.all_gather(adapter_down, 'tp', axis=1, tiled=True)  12.1 us
    all_gather x1, blocking collectives, local(): pair_all = lax.all_gather(key_value_own, 'tp', axis=1, tiled=True)  11.8 us
  transfers between devices with their start and end apart: 3, of which 1 were waited for; matrix products, arithmetic and copies ran while one was open for 4% of the time, Pallas kernels for 0%

profile of v1, /device:TPU:2, one launch (start us, length us, event | category | flops | bytes accessed | tf_op | source)
XLA Modules:
  0.0 241.8 jit_solution(9095012345948005332)
XLA Ops:
  6.5 0.0 copy-start
  6.5 0.7 all-gather.3.cloned.1.call-update
  7.3 0.0 all-gather.5.cloned.1.call-start
  7.3 0.7 all-gather.5.cloned.1.call-update
  8.0 2.0 stack.2
  10.0 20.6 %all-to-all-start = ((bf16[128,1,16,384]{3,2,1,0:T(8,128)(2,1)}), bf16[128,1,16,384]{3,2,1,0:T(8,128)(2,1)}, u32[]{:S(2)}, u32[]{:S(2)}) async-start(bf16[128,1,16,384]{3,2,1,0:T(8,128)(2,1)} %stack.2), calls=%async_computation | async-start | bytes 3145728 | tf_op jit(solution)/shard_map/all_to_all | solution.py:56
  31.2 0.7 fusion.41
  34.7 148.1 %all_gather.18 = bf16[128,16,128]{2,1,0:T(8,128)(2,1)} all-gather(bf16[1,16,128]{2,1,0:T(8,128)(2,1)S(1)} %copy-done.2), channel_id=1, replica_groups=mesh['req'=128,'tp'=4] {'req'}, dimensions={0}, use_global_device_ids=true | all-gather | bytes 528384 | tf_op jit(solution)/shard_map/all_gather | solution.py:58
  182.9 0.1 fusion.9
  183.0 1.2 multiply_cosine_fusion
  184.2 0.0 all-gather.3.cloned.1.call-done
  184.2 2.4 fusion.47
  186.6 14.7 %all-gather.5.cloned.1.call-done = bf16[128,768,32]{1,2,0:T(8,128)(2,1)} async-done(((bf16[1,768,32]{1,2,0:T(8,128)(2,1)}), bf16[128,768,32]{1,2,0:T(8,128)(2,1)}) %all-gather.5.cloned.1.call-update) | async-done | bytes 6291472 | tf_op jit(solution)/shard_map/all_gather | solution.py:54
  201.4 0.8 dynamic-slice_select_fusion
  202.2 12.1 %all_gather.17 = bf16[1,3072,32]{1,2,0:T(8,128)(2,1)S(1)} all-gather(bf16[1,768,32]{1,2,0:T(8,128)(2,1)S(1)} %dynamic-slice_select_fusion), channel_id=1, replica_groups=mesh['req'=128,'tp'=4] {'tp'}, dimensions={1}, use_global_device_ids=true | all-gather | bytes 245760 | tf_op jit(solution)/shard_map/all_gather | solution.py:64
  214.2 2.0 fusion.6
  216.2 0.0 all-to-all-done
  216.2 1.0 fusion.2
  217.2 0.2 copy.21
  217.4 0.2 copy.30
  217.6 0.2 copy.31
  217.7 0.9 convolution_multiply_fusion.2
  218.6 0.0 copy-start.4
  218.7 0.0 copy-start.1
  218.7 2.2 fusion.5
  220.9 11.8 %all_gather.19 = bf16[256,512]{1,0:T(8,128)(2,1)S(1)} all-gather(bf16[256,128]{1,0:T(8,128)(2,1)S(1)} %fusion.5), channel_id=1, replica_groups=mesh['req'=128,'tp'=4] {'tp'}, dimensions={1}, use_global_device_ids=true | all-gather | bytes 327680 | tf_op jit(solution)/shard_map/all_gather | solution.py:84
  232.7 0.6 fusion.29
  233.3 0.1 fusion.10
  233.4 0.4 fusion.46
  233.8 0.1 fusion.7
  233.9 0.3 fusion.4
  234.2 0.8 copy.26
  (23 shorter events, 0.1 us)
Async XLA Ops:
  6.5 177.7 %copy-start = (bf16[3072,384]{1,0:T(8,128)(2,1)S(1)}, bf16[3072,384]{1,0:T(8,128)(2,1)}, u32[]{:S(2)}) copy-start(bf16[3072,384]{1,0:T(8,128)(2,1)} %param.10) | copy-start | bytes 7077892
  6.5 177.7 %all-gather.3.cloned.1.call-start = ((), (), s32[]{:S(2)}) async-start(), calls=%async_computation.1 | async-start | bytes 1966080 | tf_op jit(solution)/shard_map/all_gather | solution.py:65
  7.3 194.1 %all-gather.5.cloned.1.call-start = ((), (), s32[]{:S(2)}) async-start(), calls=%async_computation.2 | async-start | bytes 6340608 | tf_op jit(solution)/shard_map/all_gather | solution.py:54
  10.0 21.2 %copy-start.9 = (s32[64]{0:T(128)S(1)}, s32[64]{0:T(128)}, u32[]{:S(2)}) copy-start(s32[64]{0:T(128)} %param.14) | copy-start | bytes 772
  10.0 24.7 %copy-start.2 = (bf16[1,16,128]{2,1,0:T(8,128)(2,1)S(1)}, bf16[1,16,128]{2,1,0:T(8,128)(2,1)}, u32[]{:S(2)}) copy-start(bf16[1,16,128]{2,1,0:T(8,128)(2,1)} %param.17) | copy-start | bytes 12292
  10.0 206.2 %all-to-all-start = ((bf16[128,1,16,384]{3,2,1,0:T(8,128)(2,1)}), bf16[128,1,16,384]{3,2,1,0:T(8,128)(2,1)}, u32[]{:S(2)}, u32[]{:S(2)}) async-start(bf16[128,1,16,384]{3,2,1,0:T(8,128)(2,1)} %stack.2), calls=%async_computation | async-start | bytes 3145728 | tf_op jit(solution)/shard_map/all_to_all | solution.py:56
  34.7 149.5 %copy-start.5 = (f32[64]{0:T(128)}, f32[64]{0:T(128)S(1)}, u32[]{:S(2)}) copy-start(f32[64]{0:T(128)S(1)} %multiply_power_fusion) | copy-start | bytes 772
  34.7 149.5 %copy-start.7 = (pred[256]{0:T(512)(128)(4,1)}, pred[256]{0:T(512)(128)(4,1)S(1)}, u32[]{:S(2)}) copy-start(pred[256]{0:T(512)(128)(4,1)S(1)} %iota_compare_fusion.1) | copy-start | bytes 772
  34.7 149.5 %copy-start.3 = (f32[256]{0:T(256)}, f32[256]{0:T(256)S(1)}, u32[]{:S(2)}) copy-start(f32[256]{0:T(256)S(1)} %iota_convert_fusion) | copy-start | bytes 3076
  218.6 14.0 %copy-start.4 = (f32[256]{0:T(256)S(1)}, f32[256]{0:T(256)}, u32[]{:S(2)}) copy-start(f32[256]{0:T(256)} %copy-done.3) | copy-start | bytes 3076
  218.6 14.0 %copy-start.6 = (f32[64]{0:T(128)S(1)}, f32[64]{0:T(128)}, u32[]{:S(2)}) copy-start(f32[64]{0:T(128)} %copy-done.5) | copy-start | bytes 772
  218.7 14.6 %copy-start.1 = (f32[256,64]{1,0:T(8,128)S(1)}, f32[256,64]{1,0:T(8,128)}, u32[]{:S(2)}) copy-start(f32[256,64]{1,0:T(8,128)} %get-tuple-element.45) | copy-start | bytes 196612
  233.3 0.6 copy-start.8
Sparse Core Ops, SparseCore 0:
  9.5 37.5 all-gather.2
  50.2 151.0 all-gather.4
